TPU v7x, 32 devices: a whole 2x2x4 slice. The times are simulated.
32 devices in a mesh: blk: 8 (over z, y), dp: 4 (over x, core).
Axes of the slice: x: 2, y: 2, z: 4, core: 2. Of those that a mesh axis runs over, the one named last changes fastest.
Arguments:
- feature_map: bfloat16 [20480, 320], P(('blk', 'dp')), may hold values from -8 to 8, as said below
- head_weight: bfloat16 [320, 1280], replicated, may hold values from -0.3125 to 0.3125
- head_shift: float32 [1280], replicated, may hold values from -0.5 to 0.5
- proj_weight: bfloat16 [1280, 256], replicated, may hold values from -0.15625 to 0.15625
Outputs:
- loss: float32 [], replicated
- grad_head: float32 [320, 1280], replicated
- grad_shift: float32 [1280], replicated
- grad_proj: float32 [1280, 256], replicated
Inputs may be any that keep to these rules, and one draw needn't show every extreme that they name: `feature_map`: features of order one.
All inputs are finite; a program needn't handle non-finite values.
Results may differ from a plain program's by a relative error of at most 0.00067.
Values may be sent and summed in bfloat16 or wider, within the bound.
No kernel may reach another device: no remote copies, remote signals or barrier semaphores. Data moves between devices by JAX's collectives and lax.ppermute only.
A program may use at most 64 MiB of HBM per device.

v0:
```python
import jax
import jax.numpy as jnp
from jax import lax
from jax.sharding import PartitionSpec as P

POS = 16


def pair_terms(rows_z, row_ids, piece, col_ids):
    sim = lax.dot_general(
        rows_z, piece, (((1,), (1,)), ((), ())), preferred_element_type=jnp.float32
    )
    kern = jnp.exp(4.0 * (sim - 1.0))
    kern = jnp.where(row_ids[:, None] == col_ids[None, :], jnp.float32(0.0), kern)
    srow = jnp.sum(kern, axis=1)
    numer = jnp.dot(kern.astype(jnp.bfloat16), piece, preferred_element_type=jnp.float32)
    return (srow, numer)


def body(feature_map, head_weight, head_shift, proj_weight):
    images = feature_map.shape[0] // POS
    channels = head_weight.shape[1]
    pre = jnp.dot(feature_map, head_weight, preferred_element_type=jnp.float32) + head_shift
    act = jax.nn.silu(pre)
    pooled = jnp.mean(act.reshape(images, POS, channels), axis=1).astype(jnp.bfloat16)
    proj = jnp.dot(pooled, proj_weight, preferred_element_type=jnp.float32)
    rnorm = jnp.sqrt(jnp.sum(proj * proj, axis=1, keepdims=True) + 1e-06)
    unit = proj / rnorm
    zed = unit.astype(jnp.bfloat16)
    batch = images * lax.axis_size("blk") * lax.axis_size("dp")
    my_ids = lax.axis_index(("blk", "dp")) * images + jnp.arange(images, dtype=jnp.int32)
    piece = lax.all_gather(zed, ("blk", "dp"), axis=0, tiled=True)
    col_ids = jnp.arange(piece.shape[0], dtype=jnp.int32)
    srow, numer = pair_terms(zed, my_ids, piece, col_ids)
    total = lax.psum(jnp.sum(srow), ("blk", "dp"))
    loss = jnp.log(total / (batch * (batch - 1.0)))
    grad_unit = batch * 8.0 / total * numer
    grad_rows = (
        (grad_unit - unit * jnp.sum(unit * grad_unit, axis=1, keepdims=True)) / rnorm
    ).astype(jnp.bfloat16)
    grad_proj = lax.dot_general(
        pooled, grad_rows, (((0,), (0,)), ((), ())), preferred_element_type=jnp.float32
    )
    grad_pooled = lax.dot_general(
        grad_rows, proj_weight, (((1,), (1,)), ((), ())), preferred_element_type=jnp.float32
    )
    grad_act = jnp.broadcast_to((grad_pooled / POS)[:, None, :], (images, POS, channels)).reshape(
        images * POS, channels
    )
    sig = jax.nn.sigmoid(pre)
    grad_pre = (grad_act * sig * (1.0 + pre * (1.0 - sig))).astype(jnp.bfloat16)
    grad_shift = jnp.sum(grad_pre.astype(jnp.float32), axis=0)
    grad_head = lax.dot_general(
        feature_map, grad_pre, (((0,), (0,)), ((), ())), preferred_element_type=jnp.float32
    )
    grad_head, grad_shift, grad_proj = lax.psum((grad_head, grad_shift, grad_proj), ("blk", "dp"))
    return (loss, grad_head, grad_shift, grad_proj)


def solution(mesh):
    return jax.shard_map(
        body,
        mesh=mesh,
        in_specs=(P(("blk", "dp"), None), P(), P(), P()),
        out_specs=(P(), P(), P(), P()),
        check_vma=False,
    )
```

profile of v0, /device:TPU:0, one launch (start us, length us, event | category | flops | bytes accessed | tf_op | source)
XLA Modules:
  0.0 256.1 jit_solution(15273268031777491178)
XLA Ops:
  7.2 0.0 copy-start
  7.2 0.0 all-reduce.3.cloned.1.call-start
  7.2 1.1 copy-done
  8.3 5.0 %fusion.2 = (f32[640,1280]{1,0:T(8,128)}, f32[640,1280]{1,0:T(8,128)}) fusion(f32[1280]{0:T(1024)} %param.6, bf16[640,320]{0,1:T(8,128)(2,1)} %param.4, bf16[320,1280]{1,0:T(8,128)(2,1)S(1)} %copy-done), kind=kOutput, calls=%fused_computation.6 | convolution fusion | flops 528384000 | bytes 7787520 | tf_op jit(solution)/shard_map/dot_general | solution.py:23
  13.3 0.0 copy-start.2
  13.3 2.5 reduce_sum.49
  15.8 0.0 copy-done.2
  15.8 0.3 multiply_reduce_fusion.1
  16.2 0.1 fusion.11
  16.3 45.0 %all_gather.3 = bf16[1280,256]{1,0:T(8,128)(2,1)S(1)} all-gather(bf16[40,256]{1,0:T(8,128)(2,1)S(1)} %fusion.11), channel_id=1, replica_groups=mesh['blk'=8,'dp'=4] {'blk','dp'}, dimensions={0}, use_global_device_ids=true | all-gather | bytes 675840 | tf_op jit(solution)/shard_map/all_gather | solution.py:32
  61.3 1.0 fusion.13
  62.3 37.0 %psum.28 = f32[]{:T(128)} all-reduce(f32[]{:T(128)} %get-tuple-element.12), channel_id=1, replica_groups=mesh['blk'=8,'dp'=4] {'blk','dp'}, use_global_device_ids=true, to_apply=%region_3.4 | all-reduce | flops 1 | bytes 8 | tf_op jit(solution)/shard_map/psum | solution.py:35
  100.0 0.0 copy-start.1
  100.0 0.3 multiply_reduce_fusion
  100.4 1.5 fusion.7
  101.8 0.0 copy-start.4
  101.8 0.4 convolution_multiply_fusion
  102.2 0.2 copy-done.1
  102.4 1.4 convert_reduce_fusion
  103.7 0.0 copy-done.4
  103.8 2.0 convolution_bitcast_fusion
  105.7 0.0 all-reduce.3.cloned.1.call-update
  106.4 41.6 %psum.30 = f32[1280]{0:T(1024)} all-reduce(f32[1280]{0:T(1024)S(1)} %get-tuple-element.6), channel_id=1, replica_groups=mesh['blk'=8,'dp'=4] {'blk','dp'}, use_global_device_ids=true, to_apply=%region_7.8 | all-reduce | flops 1280 | bytes 10240 | tf_op jit(solution)/shard_map/psum | solution.py:56
  148.0 96.3 %all-reduce.3.cloned.1.call-done = (f32[320,1280]{1,0:T(8,128)}, f32[1280,256]{1,0:T(8,128)}) async-done(((f32[320,1280]{1,0:T(8,128)}, f32[1280,256]{1,0:T(8,128)}), (f32[320,1280]{1,0:T(8,128)}, f32[1280,256]{1,0:T(8,128)})) %all-reduce.3.cloned.1.call-update) | async-done | bytes 2949136 | tf_op jit(solution)/shard_map/psum | solution.py:56
  244.3 0.0 copy-start.3
  244.3 2.8 %copy.10 = f32[320,1280]{1,0:T(8,128)} copy(f32[320,1280]{1,0:T(8,128)} %get-tuple-element.19) | data formatting | bytes 3276800
  247.1 0.0 copy-done.3
  247.1 1.1 copy.11
  (2 shorter events, 0.0 us)
Async XLA Ops:
  7.2 1.2 copy-start
  7.2 237.1 %all-reduce.3.cloned.1.call-start = ((), (), s32[]{:S(2)}) async-start(), calls=%async_computation | async-start | bytes 5898240 | tf_op jit(solution)/shard_map/psum | solution.py:56
  13.3 2.5 copy-start.2
  100.0 2.4 copy-start.1
  101.8 1.9 copy-start.4
  244.3 2.8 %copy-start.3 = (f32[1280,256]{1,0:T(8,128)S(1)}, f32[1280,256]{1,0:T(8,128)}, u32[]{:S(2)}) copy-start(f32[1280,256]{1,0:T(8,128)} %get-tuple-element.21) | copy-start | bytes 3932164
Sparse Core Ops, SparseCore 0:
  105.9 138.3 all-reduce.2
where the time goes:
time: 257 us; the launch traced here: 256 us
  blocking collectives  124 us (48%)
  waiting for transfers between devices  96.3 us (37%)
  between operations  16.6 us (6%)
  matrix products  10.4 us (4%)
  local copies, waits for them, and re-layouts  5.18 us (2%)
  other arithmetic  3.97 us (2%)
    psum x1, waiting for transfers between devices, body(): lax.psum((grad_head, grad_shift, grad_proj), ('blk', 'dp'))  96.3 us
    all_gather x1, blocking collectives, body(): piece = lax.all_gather(zed, ('blk', 'dp'), axis=0, tiled=True)  45 us
    psum x1, blocking collectives, body(): lax.psum((grad_head, grad_shift, grad_proj), ('blk', 'dp'))  41.6 us
    psum x1, blocking collectives, body(): total = lax.psum(jnp.sum(srow), ('blk', 'dp'))  37 us
    unnamed x12, local copies, waits for them, and re-layouts  5.18 us
  transfers between devices with their start and end apart: 1, of which 1 were waited for; matrix products, arithmetic and copies ran while one was open for 0% of the time, Pallas kernels for 0%

commit v1 on v0

--- a/solution.py
+++ b/solution.py
@@ -1,9 +1,39 @@
+import functools
 import jax
 import jax.numpy as jnp
 from jax import lax
 from jax.sharding import PartitionSpec as P
 
 POS = 16
+
+
+def switch_tails_for(m, dim_no):
+    m = jnp.moveaxis(m, 0, dim_no)
+    row_out = m.shape
+    built = m.reshape(
+        *row_out[:dim_no], row_out[dim_no] * row_out[dim_no + 1], *row_out[dim_no + 2 :]
+    )
+    return built
+
+
+def mark_sizes_on(xx, mesh_ax):
+    answer, kept_arr = (lax.axis_size(mesh_ax), lax.axis_index(mesh_ax))
+    new, piece_out = (xx[None], 1)
+    while piece_out < answer:
+        t_next = lax.ppermute(new, mesh_ax, perm=[(ii, ii ^ piece_out) for ii in range(answer)])
+        lower = kept_arr & piece_out == 0
+        b_now = jnp.where(lower, new, t_next)
+        new = jnp.concatenate([b_now, jnp.where(lower, t_next, new)])
+        piece_out *= 2
+    return new
+
+
+def trace_series_by_axis(z_in, target, d_out):
+    w2 = switch_tails_for(mark_sizes_on(z_in, target), d_out)
+    return w2
+
+
+feed_tasks_on = functools.partial(trace_series_by_axis, target=("blk", "dp"), d_out=0)
 
 
 def pair_terms(rows_z, row_ids, piece, col_ids):
@@ -29,7 +59,7 @@
     zed = unit.astype(jnp.bfloat16)
     batch = images * lax.axis_size("blk") * lax.axis_size("dp")
     my_ids = lax.axis_index(("blk", "dp")) * images + jnp.arange(images, dtype=jnp.int32)
-    piece = lax.all_gather(zed, ("blk", "dp"), axis=0, tiled=True)
+    piece = feed_tasks_on(zed)
     col_ids = jnp.arange(piece.shape[0], dtype=jnp.int32)
     srow, numer = pair_terms(zed, my_ids, piece, col_ids)
     total = lax.psum(jnp.sum(srow), ("blk", "dp"))

time: 257 us -> 246 us (0.957)
  blocking collectives: 124 us -> 81.4 us
  waiting for transfers between devices: 96.3 us -> 116 us
  starting transfers between devices: 0.04 us -> 11.5 us
    all_gather x1 -> x0, blocking collectives: 45 us -> none  [body(): piece = lax.all_gather(zed, ('blk', 'dp'), axis=0, tiled=True)]
    ppermute x0 -> x5, waiting for transfers between devices: none -> 19.5 us  [mark_sizes_on(): lax.ppermute(new, mesh_ax, perm=[(ii, ii ^ piece_out) for ii in range(ans...]
    ppermute x0 -> x5, starting transfers between devices: none -> 11.5 us  [mark_sizes_on(): lax.ppermute(new, mesh_ax, perm=[(ii, ii ^ piece_out) for ii in range(ans...]
    psum x1, blocking collectives: 37 us -> 40 us  [body(): total = lax.psum(jnp.sum(srow), ('blk', 'dp'))]
  transfers between devices with their start and end apart: 1 -> 6, of which waited for: 1 -> 6; matrix products, arithmetic and copies ran while one was open for 0% -> 0% of each run, Pallas kernels for 0% -> 0%
where the time goes in v1:
time: 246 us; the launch traced here: 245 us
  waiting for transfers between devices  116 us (47%)
  blocking collectives  81.4 us (33%)
  between operations  16.7 us (7%)
  starting transfers between devices  11.5 us (5%)
  matrix products  10.4 us (4%)
  local copies, waits for them, and re-layouts  5.19 us (2%)
  other arithmetic  4.29 us (2%)
    psum x1, waiting for transfers between devices, body(): lax.psum((grad_head, grad_shift, grad_proj), ('blk', 'dp'))  96.2 us
    psum x1, blocking collectives, body(): lax.psum((grad_head, grad_shift, grad_proj), ('blk', 'dp'))  41.4 us
    psum x1, blocking collectives, body(): total = lax.psum(jnp.sum(srow), ('blk', 'dp'))  40 us
    ppermute x5, waiting for transfers between devices, mark_sizes_on(): lax.ppermute(new, mesh_ax, perm=[(ii, ii ^ piece_out) for ii in range(ans...  19.5 us
    ppermute x5, starting transfers between devices, mark_sizes_on(): lax.ppermute(new, mesh_ax, perm=[(ii, ii ^ piece_out) for ii in range(ans...  11.5 us
    unnamed x12, local copies, waits for them, and re-layouts  5.19 us
    dot_general x1, matrix products, body(): jnp.dot(feature_map, head_weight, preferred_element_type=jnp.float32)  4.98 us
  transfers between devices with their start and end apart: 6, of which 6 were waited for; matrix products, arithmetic and copies ran while one was open for 0% of the time, Pallas kernels for 0%

profile of v1, /device:TPU:0, one launch (start us, length us, event | category | flops | bytes accessed | tf_op | source)
XLA Modules:
  0.0 245.2 jit_solution(12267625093980262779)
XLA Ops:
  7.2 0.0 copy-start
  7.2 0.0 all-reduce.3.cloned.1.call-start
  7.2 1.1 copy-done
  8.3 5.0 %fusion.2 = (f32[640,1280]{1,0:T(8,128)}, f32[640,1280]{1,0:T(8,128)}) fusion(f32[1280]{0:T(1024)} %param.6, bf16[640,320]{0,1:T(8,128)(2,1)} %param.4, bf16[320,1280]{1,0:T(8,128)(2,1)S(1)} %copy-done), kind=kOutput, calls=%fused_computation.6 | convolution fusion | flops 528384000 | bytes 7787520 | tf_op jit(solution)/shard_map/dot_general | solution.py:53
  13.3 2.5 %reduce_sum.49 = f32[40,1280]{1,0:T(8,128)S(1)} reduce(f32[40,16,1280]{2,1,0:T(8,128)} %bitcast.24, f32[]{:T(128)} %constant.12.clone.1), dimensions={1}, to_apply=%region_0.1 | reduce | flops 768000 | bytes 3481604 | tf_op jit(solution)/shard_map/reduce_sum | solution.py:55
  15.8 0.3 multiply_reduce_fusion.1
  16.2 0.1 convert_bitcast_fusion
  16.3 0.6 collective-permute-start
  16.8 0.8 collective-permute-done
  17.7 0.1 broadcast_select_fusion.9
  17.8 2.9 %collective-permute-start.1 = (bf16[2,40,256]{2,1,0:T(8,128)(2,1)S(1)}, bf16[2,40,256]{2,1,0:T(8,128)(2,1)S(1)}, u32[]{:S(2)}, u32[]{:S(2)}) collective-permute-start(bf16[2,40,256]{2,1,0:T(8,128)(2,1)S(1)} %pad_maximum_fusion.4), channel_id=1, source_target_pairs={{0,2},{1,3},{2,0},{3,1},{4,6},{5,7},{6,4},{7,5},{8,10},{9,11},{10,... | collective-permute-start | bytes 122888 | tf_op jit(solution)/shard_map/ppermute | solution.py:23
  20.7 2.0 collective-permute-done.1
  22.7 2.1 collective-permute-start.2
  24.8 2.4 collective-permute-done.2
  27.3 2.1 collective-permute-start.3
  29.4 3.3 %collective-permute-done.3 = bf16[8,40,256]{2,1,0:T(8,128)(2,1)S(1)} collective-permute-done((bf16[8,40,256]{2,1,0:T(8,128)(2,1)S(1)}, bf16[8,40,256]{2,1,0:T(8,128)(2,1)S(1)}, u32[]{:S(2)}, u32[]{:S(2)}) %collective-permute-start.3) | collective-permute-done | bytes 163872 | tf_op jit(solution)/shard_map/ppermute | solution.py:23
  32.8 3.8 %collective-permute-start.4 = (bf16[16,40,256]{2,1,0:T(8,128)(2,1)S(1)}, bf16[16,40,256]{2,1,0:T(8,128)(2,1)S(1)}, u32[]{:S(2)}, u32[]{:S(2)}) collective-permute-start(bf16[16,40,256]{2,1,0:T(8,128)(2,1)S(1)} %pad_maximum_fusion.1), channel_id=1, source_target_pairs={{0,16},{1,17},{2,18},{3,19},{4,20},{5,21},{6,22},{7,23},{8,24},{9,... | collective-permute-start | bytes 983048 | tf_op jit(solution)/shard_map/ppermute | solution.py:23
  36.5 10.9 %collective-permute-done.4 = bf16[16,40,256]{2,1,0:T(8,128)(2,1)S(1)} collective-permute-done((bf16[16,40,256]{2,1,0:T(8,128)(2,1)S(1)}, bf16[16,40,256]{2,1,0:T(8,128)(2,1)S(1)}, u32[]{:S(2)}, u32[]{:S(2)}) %collective-permute-start.4) | collective-permute-done | bytes 327712 | tf_op jit(solution)/shard_map/ppermute | solution.py:23
  47.5 0.1 pad_maximum_fusion
  47.6 1.0 fusion.13
  48.6 40.0 %psum.28 = f32[]{:T(128)} all-reduce(f32[]{:T(128)} %get-tuple-element.22), channel_id=1, replica_groups=mesh['blk'=8,'dp'=4] {'blk','dp'}, use_global_device_ids=true, to_apply=%region_3.4 | all-reduce | flops 1 | bytes 8 | tf_op jit(solution)/shard_map/psum | solution.py:65
  89.3 0.3 multiply_reduce_fusion
  89.6 1.5 fusion.7
  91.1 0.4 convolution_multiply_fusion
  91.4 0.2 copy-done.1
  91.7 1.4 convert_reduce_fusion
  93.0 2.0 convolution_bitcast_fusion
  95.0 0.0 all-reduce.3.cloned.1.call-update
  95.7 41.4 %psum.30 = f32[1280]{0:T(1024)} all-reduce(f32[1280]{0:T(1024)S(1)} %get-tuple-element.6), channel_id=1, replica_groups=mesh['blk'=8,'dp'=4] {'blk','dp'}, use_global_device_ids=true, to_apply=%region_7.8 | all-reduce | flops 1280 | bytes 10240 | tf_op jit(solution)/shard_map/psum | solution.py:86
  137.1 96.2 %all-reduce.3.cloned.1.call-done = (f32[320,1280]{1,0:T(8,128)}, f32[1280,256]{1,0:T(8,128)}) async-done(((f32[320,1280]{1,0:T(8,128)}, f32[1280,256]{1,0:T(8,128)}), (f32[320,1280]{1,0:T(8,128)}, f32[1280,256]{1,0:T(8,128)})) %all-reduce.3.cloned.1.call-update) | async-done | bytes 2949136 | tf_op jit(solution)/shard_map/psum | solution.py:86
  233.3 2.8 %copy.10 = f32[320,1280]{1,0:T(8,128)} copy(f32[320,1280]{1,0:T(8,128)} %get-tuple-element.29) | data formatting | bytes 3276800
  236.1 1.1 copy.11
  (17 shorter events, 0.2 us)
Async XLA Ops:
  7.2 1.2 copy-start
  7.2 226.2 %all-reduce.3.cloned.1.call-start = ((), (), s32[]{:S(2)}) async-start(), calls=%async_computation | async-start | bytes 5898240 | tf_op jit(solution)/shard_map/psum | solution.py:86
  13.3 2.5 %copy-start.2 = (bf16[1280,256]{1,0:T(8,128)(2,1)S(1)}, bf16[1280,256]{1,0:T(8,128)(2,1)}, u32[]{:S(2)}) copy-start(bf16[1280,256]{1,0:T(8,128)(2,1)} %param.7) | copy-start | bytes 1966084
  16.3 1.4 collective-permute-start
  17.8 4.9 %collective-permute-start.1 = (bf16[2,40,256]{2,1,0:T(8,128)(2,1)S(1)}, bf16[2,40,256]{2,1,0:T(8,128)(2,1)S(1)}, u32[]{:S(2)}, u32[]{:S(2)}) collective-permute-start(bf16[2,40,256]{2,1,0:T(8,128)(2,1)S(1)} %pad_maximum_fusion.4), channel_id=1, source_target_pairs={{0,2},{1,3},{2,0},{3,1},{4,6},{5,7},{6,4},{7,5},{8,10},{9,11},{10,... | collective-permute-start | bytes 122888 | tf_op jit(solution)/shard_map/ppermute | solution.py:23
  22.7 4.5 %collective-permute-start.2 = (bf16[4,40,256]{2,1,0:T(8,128)(2,1)S(1)}, bf16[4,40,256]{2,1,0:T(8,128)(2,1)S(1)}, u32[]{:S(2)}, u32[]{:S(2)}) collective-permute-start(bf16[4,40,256]{2,1,0:T(8,128)(2,1)S(1)} %pad_maximum_fusion.3), channel_id=1, source_target_pairs={{0,4},{1,5},{2,6},{3,7},{4,0},{5,1},{6,2},{7,3},{8,12},{9,13},{10,... | collective-permute-start | bytes 245768 | tf_op jit(solution)/shard_map/ppermute | solution.py:23
  27.3 5.4 %collective-permute-start.3 = (bf16[8,40,256]{2,1,0:T(8,128)(2,1)S(1)}, bf16[8,40,256]{2,1,0:T(8,128)(2,1)S(1)}, u32[]{:S(2)}, u32[]{:S(2)}) collective-permute-start(bf16[8,40,256]{2,1,0:T(8,128)(2,1)S(1)} %pad_maximum_fusion.2), channel_id=1, source_target_pairs={{0,8},{1,9},{2,10},{3,11},{4,12},{5,13},{6,14},{7,15},{8,0},{9,1},... | collective-permute-start | bytes 491528 | tf_op jit(solution)/shard_map/ppermute | solution.py:23
  32.8 14.7 %collective-permute-start.4 = (bf16[16,40,256]{2,1,0:T(8,128)(2,1)S(1)}, bf16[16,40,256]{2,1,0:T(8,128)(2,1)S(1)}, u32[]{:S(2)}, u32[]{:S(2)}) collective-permute-start(bf16[16,40,256]{2,1,0:T(8,128)(2,1)S(1)} %pad_maximum_fusion.1), channel_id=1, source_target_pairs={{0,16},{1,17},{2,18},{3,19},{4,20},{5,21},{6,22},{7,23},{8,24},{9,... | collective-permute-start | bytes 983048 | tf_op jit(solution)/shard_map/ppermute | solution.py:23
  89.3 2.4 copy-start.1
  91.1 1.9 copy-start.4
  233.3 2.8 %copy-start.3 = (f32[1280,256]{1,0:T(8,128)S(1)}, f32[1280,256]{1,0:T(8,128)}, u32[]{:S(2)}) copy-start(f32[1280,256]{1,0:T(8,128)} %get-tuple-element.31) | copy-start | bytes 3932164
Sparse Core Ops, SparseCore 0:
  95.1 138.1 all-reduce.2
